TPU v7x, 32 devices: a whole 2x2x4 slice. The times are simulated.
32 devices in a mesh: outer: 8 (over z, y), inner: 4 (over x, core).
Axes of the slice: x: 2, y: 2, z: 4, core: 2. Of those that a mesh axis runs over, the one named last changes fastest.
Arguments:
- qkv_blocks: bfloat16 [4096, 16, 512], P(('outer', 'inner')), may hold values from -4 to 4
- block_scales: bfloat16 [128, 16, 4], P(('outer', 'inner')), may hold values from 0.25 to 4
- gate_logits: bfloat16 [4096, 16, 4], P(('outer', 'inner')), may hold values from -5 to 45056
- conv_weight: float32 [4, 16, 512], P(None, 'inner'), may hold values from -3 to 3
- decay_log: float32 [32], P('inner'), may hold values from -15 to -3
- dt_bias: float32 [32], P('inner'), may hold values from -1 to 1
- norm_gain: float32 [128], replicated, may hold values from 0.5 to 1.5
Outputs:
- normed_heads: bfloat16 [4096, 32, 128], P(('outer', 'inner'))
All inputs are finite; a program needn't handle non-finite values.
Results may differ from a plain program's by a relative error of at most 0.0004.
Values may be sent and summed in bfloat16 or wider, within the bound.
No kernel may reach another device: no remote copies, remote signals or barrier semaphores. Data moves between devices by JAX's collectives and lax.ppermute only.
A program may use at most 128 MiB of HBM per device.

v0:
```python
import jax
import jax.numpy as jnp
from jax import lax
from jax.sharding import PartitionSpec as P

HD = 128
BLOCK = 128
QB = 32
CONV = 4
HIGH_PRECISION = lax.Precision.HIGHEST
EPS_NORM = 1e-06


def from_behind(value, axis, steps):
    count = lax.axis_size(axis)
    leading, last = (max(0, -steps), min(count, count - steps))
    return lax.ppermute(value, axis, [(source, source + steps) for source in range(leading, last)])


def carried_in(part, axis, combine, identity):
    place = lax.axis_index(axis)
    gathered = jax.tree.map(lambda a: lax.all_gather(a, axis), part)
    state = jax.tree.map(lambda a, e: jnp.zeros_like(a) + jnp.asarray(e, a.dtype), part, identity)

    def one(lap, state):
        return combine(
            state, jax.tree.map(lambda a: lax.dynamic_index_in_dim(a, lap, 0, False), gathered)
        )

    return lax.fori_loop(0, place, one, state)


def dequantize(blocks, scales):
    token_count = blocks.shape[0]
    head_count = blocks.shape[1]
    quarter = blocks.shape[2] // 4
    shaped = blocks.astype(jnp.float32).reshape(token_count // QB, QB, head_count, 4, quarter)
    scaled = shaped * scales.astype(jnp.float32)[:, None, :, :, None]
    return scaled.reshape(token_count, head_count, 4 * quarter)


def convolve(extended, conv_weight, token_count):
    summed = conv_weight[0] * extended[0:token_count]
    for offset in range(1, CONV):
        summed = summed + conv_weight[offset] * extended[offset : offset + token_count]
    return jax.nn.silu(summed)


def unit_rows(matrix):
    return matrix * lax.rsqrt(jnp.sum(matrix * matrix, axis=-1, keepdims=True) + EPS_NORM)


def split_heads(mixed, gate_share, decay_log, dt_bias):
    token_count = mixed.shape[0]
    value_heads = 2 * mixed.shape[1]
    block_count = token_count // BLOCK
    queries = jnp.repeat(unit_rows(mixed[:, :, :HD]), 2, axis=1)
    keys_in = jnp.repeat(unit_rows(mixed[:, :, HD : 2 * HD]), 2, axis=1)
    values_in = mixed[:, :, 2 * HD :].reshape(token_count, value_heads, HD)
    gate_values = gate_share.astype(jnp.float32)
    beta_gate = jax.nn.sigmoid(gate_values[:, :, :2].reshape(token_count, value_heads))
    raw_decay = gate_values[:, :, 2:].reshape(token_count, value_heads)
    log_decay = -jnp.exp(decay_log) * jax.nn.softplus(raw_decay + dt_bias)

    def blocked(tensor):
        return jnp.swapaxes(tensor.reshape((block_count, BLOCK) + tensor.shape[1:]), 1, 2)

    return (
        blocked(queries),
        blocked(keys_in),
        blocked(values_in),
        blocked(beta_gate),
        blocked(log_decay),
    )


def lower_inverse(strict_part, length):
    negated = -strict_part
    eye_block = jnp.eye(length, dtype=jnp.float32)
    inverse = eye_block + negated
    power = negated
    for unused_level in range((length - 1).bit_length() - 1):
        power = jnp.einsum("...ij,...jk->...ik", power, power, precision=HIGH_PRECISION)
        inverse = inverse + jnp.einsum(
            "...ij,...jk->...ik", inverse, power, precision=HIGH_PRECISION
        )
    return inverse


def block_terms(queries, keys_in, values_in, beta_gate, log_decay):
    cumulative = jnp.cumsum(log_decay, axis=-1)
    length = log_decay.shape[-1]
    row_index = lax.broadcasted_iota(jnp.int32, (length, length), 0)
    col_index = lax.broadcasted_iota(jnp.int32, (length, length), 1)
    lower_mask = row_index >= col_index
    strict = row_index > col_index
    differ = cumulative[..., :, None] - cumulative[..., None, :]
    weights = jnp.where(lower_mask, jnp.exp(jnp.where(lower_mask, differ, 0.0)), 0.0)
    key_dots = jnp.einsum("...cd,...ed->...ce", keys_in, keys_in, precision=HIGH_PRECISION)
    strict_part = jnp.where(strict, key_dots * weights * beta_gate[..., :, None], 0.0)
    growth = jnp.exp(cumulative)
    right_side = jnp.concatenate(
        [beta_gate[..., None] * values_in, (beta_gate * growth)[..., None] * keys_in], axis=-1
    )
    inverse = lower_inverse(strict_part, length)
    solved = jnp.einsum("...ce,...ed->...cd", inverse, right_side, precision=HIGH_PRECISION)
    head_width = values_in.shape[-1]
    update_part = solved[..., :head_width]
    write_part = solved[..., head_width:]
    attend = jnp.einsum("...cd,...ed->...ce", queries, keys_in, precision=HIGH_PRECISION) * weights
    final_sum = cumulative[..., -1]
    carried_keys = jnp.exp(final_sum[..., None] - cumulative)[..., None] * keys_in
    return (
        update_part,
        write_part,
        attend,
        growth[..., None] * queries,
        carried_keys,
        jnp.exp(final_sum),
    )


def block_output(update_part, write_part, attend, grown_query, current_state):
    incoming_value_rows = update_part - jnp.einsum(
        "...ck,...kv->...cv", write_part, current_state, precision=HIGH_PRECISION
    )
    result = jnp.einsum("...ck,...kv->...cv", grown_query, current_state, precision=HIGH_PRECISION)
    result = result + jnp.einsum(
        "...ce,...ev->...cv", attend, incoming_value_rows, precision=HIGH_PRECISION
    )
    return (result, incoming_value_rows)


def advance(current_state, incoming_value_rows, carried_keys, decay_total):
    return decay_total[..., None, None] * current_state + jnp.einsum(
        "...ck,...cv->...kv", carried_keys, incoming_value_rows, precision=HIGH_PRECISION
    )


def compose(earlier, later):
    trans_early, state_early = earlier
    trans_late, state_late = later
    joined_trans = jnp.einsum("hij,hjk->hik", trans_late, trans_early, precision=HIGH_PRECISION)
    joined_state = (
        jnp.einsum("hij,hjk->hik", trans_late, state_early, precision=HIGH_PRECISION) + state_late
    )
    return (joined_trans, joined_state)


def pair_update(passed_block_state, inputs):
    current_update, current_write, carried_now, decay_now = inputs
    target_values = jnp.concatenate([current_update, jnp.zeros_like(current_update)], axis=-1)
    incoming_value_rows = target_values - jnp.einsum(
        "zsg,zgj->zsj", current_write, passed_block_state, precision=HIGH_PRECISION
    )
    return advance(passed_block_state, incoming_value_rows, carried_now, decay_now)


def step_drop(passed_block_state, inputs):
    return (pair_update(passed_block_state, inputs), None)


def step_state(current_state, inputs):
    current_update, current_write, carried_now, decay_now = inputs
    incoming_value_rows = current_update - jnp.einsum(
        "zsg,zgj->zsj", current_write, current_state, precision=HIGH_PRECISION
    )
    return (advance(current_state, incoming_value_rows, carried_now, decay_now), current_state)


def local(qkv_blocks, block_scales, gate_logits, conv_weight, decay_log, dt_bias, norm_gain):
    coded_share, scale_share, gate_share = (
        lax.all_to_all(qkv_blocks, "inner", split_axis=1, concat_axis=0, tiled=True),
        lax.all_to_all(block_scales, "inner", split_axis=1, concat_axis=0, tiled=True),
        lax.all_to_all(gate_logits, "inner", split_axis=1, concat_axis=0, tiled=True),
    )
    regrouped = dequantize(coded_share, scale_share)
    token_count = regrouped.shape[0]
    previous = from_behind(regrouped[token_count - CONV + 1 :], "outer", 1)
    mixed = convolve(jnp.concatenate([previous, regrouped], axis=0), conv_weight, token_count)
    queries, keys_in, values_in, beta_gate, log_decay = split_heads(
        mixed, gate_share, decay_log, dt_bias
    )
    update_part, write_part, attend, grown_query, carried_keys, decay_total = block_terms(
        queries, keys_in, values_in, beta_gate, log_decay
    )
    head_count = queries.shape[1]
    zero_state = jnp.zeros((head_count, HD, HD), jnp.float32)
    identity = jnp.broadcast_to(jnp.eye(HD, dtype=jnp.float32), (head_count, HD, HD))
    start_pair = jnp.concatenate([zero_state, identity], axis=-1)
    sequence = (update_part, write_part, carried_keys, decay_total)
    final_pair, unused_steps = lax.scan(step_drop, start_pair, sequence)
    prefix = carried_in(
        (final_pair[..., HD:], final_pair[..., :HD]), "outer", compose, (identity, zero_state)
    )
    incoming = prefix[1]
    unused_final, starts = lax.scan(step_state, incoming, sequence)
    outputs, unused_values = block_output(update_part, write_part, attend, grown_query, starts)
    scaled = (
        outputs
        * lax.rsqrt(jnp.mean(outputs * outputs, axis=-1, keepdims=True) + EPS_NORM)
        * norm_gain
    )
    normed = scaled.astype(jnp.bfloat16)
    by_token = jnp.swapaxes(normed, 1, 2).reshape(token_count, head_count, HD)
    return lax.all_to_all(by_token, "inner", split_axis=0, concat_axis=1, tiled=True)


def solution(mesh):
    placed = (
        P(("outer", "inner"), None, None),
        P(("outer", "inner"), None, None),
        P(("outer", "inner"), None, None),
        P(None, "inner", None),
        P("inner"),
        P("inner"),
        P(),
    )
    return jax.shard_map(
        local,
        mesh=mesh,
        in_specs=placed,
        out_specs=P(("outer", "inner"), None, None),
        check_vma=False,
    )
```

profile of v0, /device:TPU:28, one launch (start us, length us, event | category | flops | bytes accessed | tf_op | source)
XLA Modules:
  0.0 353.2 jit_solution(18354611735783497234)
XLA Ops:
  7.3 6.4 %all_to_all.45 = bf16[4,16,4]{2,0,1:T(4,128)(2,1)S(1)} all-to-all(bf16[4,16,4]{2,0,1:T(4,128)(2,1)S(1)} %copy.45), channel_id=1, replica_groups=mesh['outer'=8,'inner'=4] {'inner'}, dimensions={1} | all-to-all | bytes 1024 | tf_op jit(solution)/shard_map/all_to_all | solution.py:174
  13.8 3.3 all-to-all-start
  17.0 4.1 %copy.43 = bf16[128,16,512]{2,0,1:T(8,128)(2,1)} copy(bf16[128,16,512]{2,1,0:T(8,128)(2,1)} %param.13) | data formatting | bytes 4194304 | tf_op args[0]
  21.2 3.6 %all-to-all-start.1 = ((bf16[128,16,512]{2,0,1:T(8,128)(2,1)}), bf16[128,16,512]{2,0,1:T(8,128)(2,1)S(1)}, u32[]{:S(2)}, u32[]{:S(2)}) async-start(bf16[128,16,512]{2,0,1:T(8,128)(2,1)} %copy.43), calls=%async_computation.1 | async-start | bytes 4194304 | tf_op jit(solution)/shard_map/all_to_all | solution.py:173
  25.6 2.6 mul.179
  28.2 5.5 %mul.180 = f32[512,4,512]{2,0,1:T(8,128)} reshape(f32[16,32,4,4,128]{4,3,1,0,2:T(4,128)} %mul.179) | data formatting | bytes 8388608 | tf_op jit(solution)/shard_map/mul | solution.py:38
  35.2 15.2 %all-to-all-done.1 = bf16[128,16,512]{2,0,1:T(8,128)(2,1)S(1)} async-done(((bf16[128,16,512]{2,0,1:T(8,128)(2,1)}), bf16[128,16,512]{2,0,1:T(8,128)(2,1)S(1)}, u32[]{:S(2)}, u32[]{:S(2)}) %all-to-all-start.1) | async-done | bytes 2097184 | tf_op jit(solution)/shard_map/all_to_all | solution.py:173
  55.7 4.4 %collective-permute-done = f32[3,4,512]{2,0,1:T(4,128)S(1)} collective-permute-done((f32[3,4,512]{2,0,1:T(4,128)S(1)}, f32[3,4,512]{2,0,1:T(4,128)S(1)}, u32[]{:S(2)}, u32[]{:S(2)}) %collective-permute-start) | collective-permute-done | bytes 24608 | tf_op jit(solution)/shard_map/ppermute | solution.py:17
  60.1 2.5 divide_multiply_fusion
  65.3 4.7 %select_negate_fusion = f32[4,8,128,128]{3,2,1,0:T(8,128)S(1)} fusion(f32[4,128,8,128]{3,1,0,2:T(8,128)S(1)} %bitcast.175, f32[4,8,128]{2,1,0:T(8,128)S(1)} %bitcast.187, f32[4,8,128]{2,1,0:T(8,128)S(1)} %reduce_window_sum.11, pred[128,128]{1,0:T(8,128)(4,1)S(1)} %get-tuple-element.232, pred[128,128]{1,0:T(8,128)(4,1)S(1)} %get-tuple-element.233), kind=kOutput, calls=%fused_computation.62 | convolution fusion | flops 808976384 | bytes 4259840 | tf_op jit(solution)/shard_map/...cd,...ed->...ce/dot_general | solution.py:99
  72.2 2.6 add_add_fusion
  77.0 2.6 fusion.78
  90.4 3.6 %fusion.82 = f32[4,8,128,128]{3,2,1,0:T(8,128)} fusion(f32[4,8,128,128]{3,2,1,0:T(8,128)S(1)} %fusion.81), kind=kOutput, calls=%fused_computation.125 | convolution fusion | flops 805306368 | bytes 4194304 | tf_op jit(solution)/shard_map/...ij,...jk->...ik/dot_general | solution.py:83
  94.0 3.7 %convolution_add_fusion.3 = f32[4,8,128,128]{3,2,1,0:T(8,128)} fusion(f32[4,8,128,128]{3,2,1,0:T(8,128)S(1)} %fusion.81, f32[4,8,128,128]{3,2,1,0:T(8,128)S(1)} %convolution_add_fusion.4, f32[4,8,128,128]{3,2,1,0:T(8,128)S(1)} %fusion.80), kind=kOutput, calls=%fused_computation.67 | convolution fusion | flops 806354944 | bytes 8388608 | tf_op jit(solution)/shard_map/...ij,...jk->...ik/dot_general | solution.py:84
  97.7 2.7 copy.50
  100.4 3.0 reshape_reshape.11
  110.9 4.3 %fusion.25 = f32[4,8,128,256]{3,2,1,0:T(8,128)S(1)} fusion(f32[4,8,128,128]{3,2,1,0:T(8,128)S(1)} %get-tuple-element.215, f32[4,8,128,128]{3,2,1,0:T(8,128)S(1)} %bitcast_multiply_fusion.2, f32[4,8,128,128]{3,2,1,0:T(8,128)S(1)} %copy-done.7, f32[4,8,128,128]{3,2,1,0:T(8,128)S(1)} %fusion.83), kind=kOutput, calls=%fused_computation.37 | convolution fusion | flops 1612185600 | bytes 12582912 | tf_op jit(solution)/shard_map/...ce,...ed->...cd/dot_general | solution.py:106
  117.9 2.9 copy.52
  120.8 18.2 %while.37 = (s32[]{:T(128)}, f32[8,128,256]{2,1,0:T(8,128)S(1)}, f32[4,8]{1,0:T(4,128)S(1)}, f32[4,8,128,128]{2,3,1,0:T(8,128)}, f32[4,8,128,128]{3,2,1,0:T(8,128)S(1)}, /*index=5*/f32[4,8,128,128]{3,2,1,0:T(8,128)}) while((s32[]{:T(128)}, f32[8,128,256]{2,1,0:T(8,128)S(1)}, f32[4,8]{1,0:T(4,128)S(1)}, ...), condition=%wide.region_4.5_spmd.clone, body=%wide.region_3.4_spmd.sunk.clone | while | flops 806092800 | bytes 7865517 | solution.py:192
  122.9 2.4 convolution_add_fusion.11
  127.5 2.4 convolution_add_fusion.11
  132.0 2.4 convolution_add_fusion.11
  136.6 2.4 convolution_add_fusion.11
  143.7 5.8 %fusion.31 = f32[4,8,128,128]{3,2,1,0:T(8,128)} fusion(f32[4,8,128,128]{3,2,0,1:T(8,128)S(1)} %bitcast.178, f32[4,128,8,128]{3,1,0,2:T(8,128)S(1)} %bitcast.177), kind=kOutput, calls=%fused_computation.48 | convolution fusion | flops 805306368 | bytes 6291456 | tf_op jit(solution)/shard_map/...cd,...ed->...ce/dot_general | solution.py:110
  149.5 61.5 %all-gather.5.cloned.1.call-done = f32[64,128,128]{2,1,0:T(8,128)} async-done(((f32[8,128,128]{2,1,0:T(8,128)}), f32[64,128,128]{2,1,0:T(8,128)}) %all-gather.5.cloned.1.call-update) | async-done | bytes 4194320 | tf_op jit(solution)/shard_map/all_gather | solution.py:22
  211.0 73.8 %all-gather.7.cloned.1.call-done = f32[64,128,128]{2,1,0:T(8,128)} async-done(((f32[8,128,128]{2,1,0:T(8,128)}), f32[64,128,128]{2,1,0:T(8,128)}) %all-gather.7.cloned.1.call-update) | async-done | bytes 4194320 | tf_op jit(solution)/shard_map/all_gather | solution.py:22
  284.8 13.5 %while.38 = (s32[]{:T(128)}, f32[8,128,128]{2,1,0:T(8,128)S(1)}, s32[]{:T(128)}, f32[8,8,128,128]{3,2,1,0:T(8,128)}, f32[8,8,128,128]{3,2,1,0:T(8,128)}) while((s32[]{:T(128)}, f32[8,128,128]{2,1,0:T(8,128)S(1)}, s32[]{:T(128)}, f32[8,8,128,128]{3,2,1,0:T(8,128)}, f32[8,8,128,128]{3,2,1,0:T(8,128)}) %tuple.95), condition=%wide.region_6.7_spmd.clone, body=%wide.region_5.6_spmd.sunk.clone | while | flops 201457664 | bytes 3146847 | solution.py:30
  298.3 18.0 %while.39 = (s32[]{:T(128)}, f32[8,128,128]{2,1,0:T(8,128)S(1)}, f32[4,8,128,128]{3,2,1,0:T(8,128)}, f32[4,8]{1,0:T(4,128)S(1)}, f32[4,8,128,128]{2,3,1,0:T(8,12...) while((s32[]{:T(128)}, f32[8,128,128]{2,1,0:T(8,128)S(1)}, ...), condition=%wide.region_8.9_spmd.clone, body=%wide.region_7.8_spmd.sunk.clone | while | flops 403046400 | bytes 5245105 | solution.py:197
  316.4 4.5 %fusion.69 = f32[4,8,128,128]{3,2,1,0:T(8,128)S(1)} fusion(f32[4,8,128,128]{3,2,1,0:T(8,128)} %get-tuple-element.120, f32[4,8,128,256]{3,2,1,0:T(8,128)} %copy-done), kind=kOutput, calls=%fused_computation.112 | convolution fusion | flops 805306368 | bytes 6291456 | tf_op jit(solution)/shard_map/...ck,...kv->...cv/dot_general | solution.py:124
  321.0 2.6 fusion.38
  323.6 2.8 multiply_reduce_fusion
  327.8 17.0 %all_to_all.46 = bf16[512,8,128]{2,1,0:T(8,128)(2,1)S(1)} all-to-all(bf16[512,8,128]{2,1,0:T(8,128)(2,1)S(1)} %bitcast.181), channel_id=1, replica_groups=mesh['outer'=8,'inner'=4] {'inner'}, dimensions={0} | all-to-all | bytes 2097152 | tf_op jit(solution)/shard_map/all_to_all | solution.py:206
  (131 shorter events, 82.8 us)
Async XLA Ops:
  13.8 7.4 %all-to-all-start = ((bf16[128,16,4]{0,2,1:T(4,128)(2,1)}), bf16[128,16,4]{0,2,1:T(4,128)(2,1)S(1)}, u32[]{:S(2)}, u32[]{:S(2)}) async-start(bf16[128,16,4]{0,2,1:T(4,128)(2,1)} %param.15), calls=%async_computation | async-start | bytes 32768 | tf_op jit(solution)/shard_map/all_to_all | solution.py:175
  21.2 29.3 %all-to-all-start.1 = ((bf16[128,16,512]{2,0,1:T(8,128)(2,1)}), bf16[128,16,512]{2,0,1:T(8,128)(2,1)S(1)}, u32[]{:S(2)}, u32[]{:S(2)}) async-start(bf16[128,16,512]{2,0,1:T(8,128)(2,1)} %copy.43), calls=%async_computation.1 | async-start | bytes 4194304 | tf_op jit(solution)/shard_map/all_to_all | solution.py:173
  24.8 0.7 copy-start.15
  24.8 0.8 copy-start.12
  24.8 186.2 %all-gather.5.cloned.1.call-start = ((), (), s32[]{:S(2)}) async-start(), calls=%async_computation.4 | async-start | bytes 4718592 | tf_op jit(solution)/shard_map/all_gather | solution.py:22
  28.2 5.6 %copy-start.13 = (f32[8]{0:T(128)S(1)}, f32[8]{0:T(128)}, u32[]{:S(2)}) copy-start(f32[8]{0:T(128)} %param.18) | copy-start | bytes 100
  51.0 2.2 copy-start.8
  54.3 5.8 %collective-permute-start = (f32[3,4,512]{2,0,1:T(4,128)S(1)}, f32[3,4,512]{2,0,1:T(4,128)S(1)}, u32[]{:S(2)}, u32[]{:S(2)}) collective-permute-start(f32[3,4,512]{2,0,1:T(4,128)S(1)} %slice.73), channel_id=1, source_target_pairs={{0,4},{4,8},{8,12},{12,16},{16,20},{20,24},{24,28},{1,5},{5,9},{9,... | collective-permute-start | bytes 73736 | tf_op jit(solution)/shard_map/ppermute | solution.py:17
  62.6 14.4 %copy-start.2 = (f32[512,4,512]{2,0,1:T(8,128)}, f32[512,4,512]{2,0,1:T(8,128)S(1)}, u32[]{:S(2)}) copy-start(f32[512,4,512]{2,0,1:T(8,128)S(1)} %divide_multiply_fusion) | copy-start | bytes 12582916
  65.3 43.3 %copy-start.3 = (f32[512,4,2,128]{3,0,2,1:T(8,128)}, f32[512,4,2,128]{3,0,2,1:T(8,128)S(1)}, u32[]{:S(2)}) copy-start(f32[512,4,2,128]{3,0,2,1:T(8,128)S(1)} %broadcast_in_dim.49) | copy-start | bytes 6291460
  94.0 3.7 %slice-start = ((f32[512,4,512]{2,0,1:T(8,128)}), f32[512,4,256]{2,0,1:T(8,128)S(1)}, s32[]{:S(2)}) async-start(f32[512,4,512]{2,0,1:T(8,128)} %copy-done.2), calls=%async_computation.6 | async-start | bytes 4194304 | tf_op jit(solution)/shard_map/slice | solution.py:59
  103.4 2.3 copy-start.7
  103.4 2.9 copy-start.9
  115.3 2.6 copy-start
  140.1 144.7 %all-gather.7.cloned.1.call-start = ((), (), s32[]{:S(2)}) async-start(), calls=%async_computation.5 | async-start | bytes 4718592 | tf_op jit(solution)/shard_map/all_gather | solution.py:22
  140.8 2.9 copy-start.4
  142.4 1.3 copy-start.5
  316.4 4.5 %copy-start.1 = (f32[4,8,128,256]{3,2,1,0:T(8,128)S(1)}, f32[4,8,128,256]{3,2,1,0:T(8,128)}, u32[]{:S(2)}) copy-start(f32[4,8,128,256]{3,2,1,0:T(8,128)} %copy-done) | copy-start | bytes 12582916
  316.4 4.5 %copy-start.10 = (f32[4,8,128,128]{3,2,1,0:T(8,128)S(1)}, f32[4,8,128,128]{3,2,1,0:T(8,128)}, u32[]{:S(2)}) copy-start(f32[4,8,128,128]{3,2,1,0:T(8,128)} %fusion.31) | copy-start | bytes 6291460
  320.9 2.6 copy-start.6
  320.9 2.6 copy-start.11
  323.6 2.8 copy-start.14
Sparse Core Ops, SparseCore 0:
  140.2 70.7 all-gather.4
  213.1 71.6 all-gather.6
where the time goes:
time: 360 us; the launch traced here: 353 us
  waiting for transfers between devices  156 us (43%)
  matrix products  99.6 us (28%)
  local copies, waits for them, and re-layouts  37.8 us (10%)
  blocking collectives  23.4 us (6%)
  between operations  14.4 us (4%)
  other arithmetic  13.4 us (4%)
  starting transfers between devices  8.24 us (2%)
    all_gather x2, waiting for transfers between devices, carried_in(): gathered = jax.tree.map(lambda a: lax.all_gather(a, axis), part)  135 us
    dot_general x8, matrix products, advance(): jnp.einsum('...ck,...cv->...kv', carried_keys, incoming_value_rows, preci...  17 us
    all_to_all x1, blocking collectives, local(): lax.all_to_all(by_token, 'inner', split_axis=0, concat_axis=1, tiled=True)  17 us
    dot_general x6, matrix products, lower_inverse(): jnp.einsum('...ij,...jk->...ik', inverse, power, precision=HIGH_PRECISION)  15.3 us
    all_to_all x1, waiting for transfers between devices, local(): lax.all_to_all(qkv_blocks, 'inner', split_axis=1, concat_axis=0, tiled=True)  15.2 us
    dot_general x6, matrix products, lower_inverse(): jnp.einsum('...ij,...jk->...ik', power, power, precision=HIGH_PRECISION)  14.5 us
    dot_general x7, matrix products, compose(): jnp.einsum('hij,hjk->hik', trans_late, state_early, precision=HIGH_PRECIS...  13 us
    unnamed x34, local copies, waits for them, and re-layouts  9.55 us
  transfers between devices with their start and end apart: 5, of which 4 were waited for; matrix products, arithmetic and copies ran while one was open for 6% of the time, Pallas kernels for 0%

commit v1 on v0

--- a/solution.py
+++ b/solution.py
@@ -203,7 +203,12 @@
     )
     normed = scaled.astype(jnp.bfloat16)
     by_token = jnp.swapaxes(normed, 1, 2).reshape(token_count, head_count, HD)
-    return lax.all_to_all(by_token, "inner", split_axis=0, concat_axis=1, tiled=True)
+    return jnp.concatenate(
+        lax.all_to_all(
+            jnp.stack(jnp.split(by_token, lax.axis_size("inner"), axis=0)), "inner", 0, 0
+        ),
+        axis=1,
+    )
 
 
 def solution(mesh):

time: 360 us -> 363 us (level)
  no operation moved by 1% of the time
where the time goes in v1:
time: 363 us; the launch traced here: 356 us
  waiting for transfers between devices  156 us (43%)
  matrix products  103 us (28%)
  local copies, waits for them, and re-layouts  37.6 us (10%)
  blocking collectives  23.4 us (6%)
  between operations  14.4 us (4%)
  other arithmetic  13.1 us (4%)
  starting transfers between devices  8.24 us (2%)
    all_gather x2, waiting for transfers between devices, carried_in(): gathered = jax.tree.map(lambda a: lax.all_gather(a, axis), part)  135 us
    dot_general x8, matrix products, advance(): jnp.einsum('...ck,...cv->...kv', carried_keys, incoming_value_rows, preci...  17 us
    all_to_all x1, blocking collectives, local(): lax.all_to_all(jnp.stack(jnp.split(by_token, lax.axis_size('inner'), axis...  17 us
    dot_general x6, matrix products, lower_inverse(): jnp.einsum('...ij,...jk->...ik', inverse, power, precision=HIGH_PRECISION)  15.3 us
    all_to_all x1, waiting for transfers between devices, local(): lax.all_to_all(qkv_blocks, 'inner', split_axis=1, concat_axis=0, tiled=True)  15.2 us
    dot_general x6, matrix products, lower_inverse(): jnp.einsum('...ij,...jk->...ik', power, power, precision=HIGH_PRECISION)  14.5 us
    dot_general x7, matrix products, compose(): jnp.einsum('hij,hjk->hik', trans_late, state_early, precision=HIGH_PRECIS...  13 us
    unnamed x34, local copies, waits for them, and re-layouts  9.55 us
  transfers between devices with their start and end apart: 5, of which 4 were waited for; matrix products, arithmetic and copies ran while one was open for 6% of the time, Pallas kernels for 0%

profile of v1, /device:TPU:28, one launch (start us, length us, event | category | flops | bytes accessed | tf_op | source)
XLA Modules:
  0.0 355.7 jit_solution(11261421237030955748)
XLA Ops:
  7.3 6.4 %all_to_all.32 = bf16[4,16,4]{2,0,1:T(4,128)(2,1)S(1)} all-to-all(bf16[4,16,4]{2,0,1:T(4,128)(2,1)S(1)} %copy.51), channel_id=1, replica_groups=mesh['outer'=8,'inner'=4] {'inner'}, dimensions={1} | all-to-all | bytes 1024 | tf_op jit(solution)/shard_map/all_to_all | solution.py:174
  13.8 3.3 all-to-all-start
  17.0 4.1 %copy.49 = bf16[128,16,512]{2,0,1:T(8,128)(2,1)} copy(bf16[128,16,512]{2,1,0:T(8,128)(2,1)} %param.13) | data formatting | bytes 4194304 | tf_op args[0]
  21.2 3.6 %all-to-all-start.1 = ((bf16[128,16,512]{2,0,1:T(8,128)(2,1)}), bf16[128,16,512]{2,0,1:T(8,128)(2,1)S(1)}, u32[]{:S(2)}, u32[]{:S(2)}) async-start(bf16[128,16,512]{2,0,1:T(8,128)(2,1)} %copy.49), calls=%async_computation.1 | async-start | bytes 4194304 | tf_op jit(solution)/shard_map/all_to_all | solution.py:173
  25.6 2.6 mul.179
  28.2 5.5 %mul.180 = f32[512,4,512]{2,0,1:T(8,128)} reshape(f32[16,32,4,4,128]{4,3,1,0,2:T(4,128)} %mul.179) | data formatting | bytes 8388608 | tf_op jit(solution)/shard_map/mul | solution.py:38
  35.2 15.2 %all-to-all-done.1 = bf16[128,16,512]{2,0,1:T(8,128)(2,1)S(1)} async-done(((bf16[128,16,512]{2,0,1:T(8,128)(2,1)}), bf16[128,16,512]{2,0,1:T(8,128)(2,1)S(1)}, u32[]{:S(2)}, u32[]{:S(2)}) %all-to-all-start.1) | async-done | bytes 2097184 | tf_op jit(solution)/shard_map/all_to_all | solution.py:173
  55.7 4.4 %collective-permute-done = f32[3,4,512]{2,0,1:T(4,128)S(1)} collective-permute-done((f32[3,4,512]{2,0,1:T(4,128)S(1)}, f32[3,4,512]{2,0,1:T(4,128)S(1)}, u32[]{:S(2)}, u32[]{:S(2)}) %collective-permute-start) | collective-permute-done | bytes 24608 | tf_op jit(solution)/shard_map/ppermute | solution.py:17
  60.1 2.5 divide_multiply_fusion
  65.3 4.7 %select_negate_fusion = f32[4,8,128,128]{3,2,1,0:T(8,128)S(1)} fusion(f32[4,128,8,128]{3,1,0,2:T(8,128)S(1)} %bitcast.171, f32[4,8,128]{2,1,0:T(8,128)S(1)} %bitcast.182, f32[4,8,128]{2,1,0:T(8,128)S(1)} %reduce_window_sum.11, pred[128,128]{1,0:T(8,128)(4,1)S(1)} %get-tuple-element.232, pred[128,128]{1,0:T(8,128)(4,1)S(1)} %get-tuple-element.233), kind=kOutput, calls=%fused_computation.62 | convolution fusion | flops 808976384 | bytes 4259840 | tf_op jit(solution)/shard_map/...cd,...ed->...ce/dot_general | solution.py:99
  72.2 2.6 add_add_fusion
  77.0 2.6 fusion.78
  90.4 3.6 %fusion.82 = f32[4,8,128,128]{3,2,1,0:T(8,128)} fusion(f32[4,8,128,128]{3,2,1,0:T(8,128)S(1)} %fusion.81), kind=kOutput, calls=%fused_computation.124 | convolution fusion | flops 805306368 | bytes 4194304 | tf_op jit(solution)/shard_map/...ij,...jk->...ik/dot_general | solution.py:83
  94.0 3.7 %convolution_add_fusion.3 = f32[4,8,128,128]{3,2,1,0:T(8,128)} fusion(f32[4,8,128,128]{3,2,1,0:T(8,128)S(1)} %fusion.81, f32[4,8,128,128]{3,2,1,0:T(8,128)S(1)} %convolution_add_fusion.4, f32[4,8,128,128]{3,2,1,0:T(8,128)S(1)} %fusion.80), kind=kOutput, calls=%fused_computation.67 | convolution fusion | flops 806354944 | bytes 8388608 | tf_op jit(solution)/shard_map/...ij,...jk->...ik/dot_general | solution.py:84
  97.7 2.7 copy.56
  100.4 3.0 reshape_reshape.11
  110.9 4.3 %fusion.25 = f32[4,8,128,256]{3,2,1,0:T(8,128)S(1)} fusion(f32[4,8,128,128]{3,2,1,0:T(8,128)S(1)} %get-tuple-element.215, f32[4,8,128,128]{3,2,1,0:T(8,128)S(1)} %bitcast_multiply_fusion.2, f32[4,8,128,128]{3,2,1,0:T(8,128)S(1)} %copy-done.7, f32[4,8,128,128]{3,2,1,0:T(8,128)S(1)} %fusion.83), kind=kOutput, calls=%fused_computation.37 | convolution fusion | flops 1612185600 | bytes 12582912 | tf_op jit(solution)/shard_map/...ce,...ed->...cd/dot_general | solution.py:106
  117.9 2.9 copy.58
  120.8 18.2 %while.37 = (s32[]{:T(128)}, f32[8,128,256]{2,1,0:T(8,128)S(1)}, f32[4,8]{1,0:T(4,128)S(1)}, f32[4,8,128,128]{2,3,1,0:T(8,128)}, f32[4,8,128,128]{3,2,1,0:T(8,128)S(1)}, /*index=5*/f32[4,8,128,128]{3,2,1,0:T(8,128)}) while((s32[]{:T(128)}, f32[8,128,256]{2,1,0:T(8,128)S(1)}, f32[4,8]{1,0:T(4,128)S(1)}, ...), condition=%wide.region_4.5_spmd.clone, body=%wide.region_3.4_spmd.sunk.clone | while | flops 806092800 | bytes 7865517 | solution.py:192
  122.9 2.4 convolution_add_fusion.11
  127.5 2.4 convolution_add_fusion.11
  132.0 2.4 convolution_add_fusion.11
  136.6 2.4 convolution_add_fusion.11
  143.7 5.8 %fusion.31 = f32[4,8,128,128]{3,2,1,0:T(8,128)} fusion(f32[4,8,128,128]{3,2,0,1:T(8,128)S(1)} %bitcast.174, f32[4,128,8,128]{3,1,0,2:T(8,128)S(1)} %bitcast.173), kind=kOutput, calls=%fused_computation.48 | convolution fusion | flops 805306368 | bytes 6291456 | tf_op jit(solution)/shard_map/...cd,...ed->...ce/dot_general | solution.py:110
  149.5 61.5 %all-gather.5.cloned.1.call-done = f32[64,128,128]{2,1,0:T(8,128)} async-done(((f32[8,128,128]{2,1,0:T(8,128)}), f32[64,128,128]{2,1,0:T(8,128)}) %all-gather.5.cloned.1.call-update) | async-done | bytes 4194320 | tf_op jit(solution)/shard_map/all_gather | solution.py:22
  211.0 73.8 %all-gather.7.cloned.1.call-done = f32[64,128,128]{2,1,0:T(8,128)} async-done(((f32[8,128,128]{2,1,0:T(8,128)}), f32[64,128,128]{2,1,0:T(8,128)}) %all-gather.7.cloned.1.call-update) | async-done | bytes 4194320 | tf_op jit(solution)/shard_map/all_gather | solution.py:22
  284.8 13.5 %while.38 = (s32[]{:T(128)}, f32[8,128,128]{2,1,0:T(8,128)S(1)}, s32[]{:T(128)}, f32[8,8,128,128]{3,2,1,0:T(8,128)}, f32[8,8,128,128]{3,2,1,0:T(8,128)}) while((s32[]{:T(128)}, f32[8,128,128]{2,1,0:T(8,128)S(1)}, s32[]{:T(128)}, f32[8,8,128,128]{3,2,1,0:T(8,128)}, f32[8,8,128,128]{3,2,1,0:T(8,128)}) %tuple.95), condition=%wide.region_6.7_spmd.clone, body=%wide.region_5.6_spmd.sunk.clone | while | flops 201457664 | bytes 3146847 | solution.py:30
  298.3 18.0 %while.39 = (s32[]{:T(128)}, f32[8,128,128]{2,1,0:T(8,128)S(1)}, f32[4,8,128,128]{3,2,1,0:T(8,128)}, f32[4,8]{1,0:T(4,128)S(1)}, f32[4,8,128,128]{2,3,1,0:T(8,12...) while((s32[]{:T(128)}, f32[8,128,128]{2,1,0:T(8,128)S(1)}, ...), condition=%wide.region_8.9_spmd.clone, body=%wide.region_7.8_spmd.sunk.clone | while | flops 403046400 | bytes 5245105 | solution.py:197
  316.4 4.5 %fusion.69 = f32[4,8,128,128]{3,2,1,0:T(8,128)S(1)} fusion(f32[4,8,128,128]{3,2,1,0:T(8,128)} %get-tuple-element.120, f32[4,8,128,256]{3,2,1,0:T(8,128)} %copy-done), kind=kOutput, calls=%fused_computation.111 | convolution fusion | flops 805306368 | bytes 6291456 | tf_op jit(solution)/shard_map/...ck,...kv->...cv/dot_general | solution.py:124
  321.0 4.2 %fusion.38 = f32[4,8,128,128]{2,3,1,0:T(8,128)S(1)} fusion(f32[4,8,128,128]{3,2,1,0:T(8,128)S(1)} %fusion.69, f32[4,8,128,128]{3,2,1,0:T(8,128)S(1)} %copy-done.10, f32[4,8,128]{2,1,0:T(8,128)S(1)} %reduce_window_sum.11, pred[128,128]{1,0:T(8,128)(4,1)S(1)} %get-tuple-element.232, f32[4,8,128,256]{3,2,1,0:T(8,128)S(1)} %copy-done.1), kind=kOutput, calls=%fused_computation.58 | convolution fusion | flops 807927808 | bytes 8437760 | tf_op jit(solution)/shard_map/...ce,...ev->...cv/dot_general | solution.py:128
  325.1 4.2 %multiply_reduce_fusion = (f32[4,8,128]{2,1,0:T(8,128)S(1)}, f32[4,8,128,128]{2,3,1,0:T(8,128)S(1)}) fusion(f32[4,8,128,128]{2,3,1,0:T(8,128)S(1)} %fusion.38, f32[4,8,128,128]{3,2,1,0:T(8,128)S(1)} %copy-done.11, f32[4,8,128,128]{3,2,0,1:T(8,128)S(1)} %bitcast.175, f32[4,8,128]{2,0,1:T(4,128)S(1)} %copy.48), kind=kOutput, calls=%fused_computation.57 | convolution fusion | flops 807399424 | bytes 8421376 | tf_op jit(solution)/shard_map/...ck,...kv->...cv/dot_general | solution.py:127
  329.7 17.0 %all_to_all.33 = bf16[4,128,8,128]{1,3,2,0:T(8,128)(2,1)S(1)} all-to-all(bf16[4,128,8,128]{1,3,2,0:T(8,128)(2,1)S(1)} %fusion.30), channel_id=1, replica_groups=mesh['outer'=8,'inner'=4] {'inner'}, dimensions={0} | all-to-all | bytes 2097152 | tf_op jit(solution)/shard_map/all_to_all | solution.py:207
  (130 shorter events, 82.3 us)
Async XLA Ops:
  13.8 7.4 %all-to-all-start = ((bf16[128,16,4]{0,2,1:T(4,128)(2,1)}), bf16[128,16,4]{0,2,1:T(4,128)(2,1)S(1)}, u32[]{:S(2)}, u32[]{:S(2)}) async-start(bf16[128,16,4]{0,2,1:T(4,128)(2,1)} %param.15), calls=%async_computation | async-start | bytes 32768 | tf_op jit(solution)/shard_map/all_to_all | solution.py:175
  21.2 29.3 %all-to-all-start.1 = ((bf16[128,16,512]{2,0,1:T(8,128)(2,1)}), bf16[128,16,512]{2,0,1:T(8,128)(2,1)S(1)}, u32[]{:S(2)}, u32[]{:S(2)}) async-start(bf16[128,16,512]{2,0,1:T(8,128)(2,1)} %copy.49), calls=%async_computation.1 | async-start | bytes 4194304 | tf_op jit(solution)/shard_map/all_to_all | solution.py:173
  24.8 0.7 copy-start.15
  24.8 0.8 copy-start.12
  24.8 186.2 %all-gather.5.cloned.1.call-start = ((), (), s32[]{:S(2)}) async-start(), calls=%async_computation.4 | async-start | bytes 4718592 | tf_op jit(solution)/shard_map/all_gather | solution.py:22
  28.2 5.6 %copy-start.13 = (f32[8]{0:T(128)S(1)}, f32[8]{0:T(128)}, u32[]{:S(2)}) copy-start(f32[8]{0:T(128)} %param.18) | copy-start | bytes 100
  51.0 2.2 copy-start.8
  54.3 5.8 %collective-permute-start = (f32[3,4,512]{2,0,1:T(4,128)S(1)}, f32[3,4,512]{2,0,1:T(4,128)S(1)}, u32[]{:S(2)}, u32[]{:S(2)}) collective-permute-start(f32[3,4,512]{2,0,1:T(4,128)S(1)} %slice.78), channel_id=1, source_target_pairs={{0,4},{4,8},{8,12},{12,16},{16,20},{20,24},{24,28},{1,5},{5,9},{9,... | collective-permute-start | bytes 73736 | tf_op jit(solution)/shard_map/ppermute | solution.py:17
  62.6 14.4 %copy-start.2 = (f32[512,4,512]{2,0,1:T(8,128)}, f32[512,4,512]{2,0,1:T(8,128)S(1)}, u32[]{:S(2)}) copy-start(f32[512,4,512]{2,0,1:T(8,128)S(1)} %divide_multiply_fusion) | copy-start | bytes 12582916
  65.3 43.3 %copy-start.3 = (f32[512,4,2,128]{3,0,2,1:T(8,128)}, f32[512,4,2,128]{3,0,2,1:T(8,128)S(1)}, u32[]{:S(2)}) copy-start(f32[512,4,2,128]{3,0,2,1:T(8,128)S(1)} %broadcast_in_dim.49) | copy-start | bytes 6291460
  94.0 3.7 %slice-start = ((f32[512,4,512]{2,0,1:T(8,128)}), f32[512,4,256]{2,0,1:T(8,128)S(1)}, s32[]{:S(2)}) async-start(f32[512,4,512]{2,0,1:T(8,128)} %copy-done.2), calls=%async_computation.6 | async-start | bytes 4194304 | tf_op jit(solution)/shard_map/slice | solution.py:59
  103.4 2.3 copy-start.7
  103.4 2.9 copy-start.9
  115.3 2.6 copy-start
  140.1 144.7 %all-gather.7.cloned.1.call-start = ((), (), s32[]{:S(2)}) async-start(), calls=%async_computation.5 | async-start | bytes 4718592 | tf_op jit(solution)/shard_map/all_gather | solution.py:22
  140.8 2.9 copy-start.4
  142.4 1.3 copy-start.5
  316.4 4.5 %copy-start.1 = (f32[4,8,128,256]{3,2,1,0:T(8,128)S(1)}, f32[4,8,128,256]{3,2,1,0:T(8,128)}, u32[]{:S(2)}) copy-start(f32[4,8,128,256]{3,2,1,0:T(8,128)} %copy-done) | copy-start | bytes 12582916
  316.4 4.5 %copy-start.10 = (f32[4,8,128,128]{3,2,1,0:T(8,128)S(1)}, f32[4,8,128,128]{3,2,1,0:T(8,128)}, u32[]{:S(2)}) copy-start(f32[4,8,128,128]{3,2,1,0:T(8,128)} %fusion.31) | copy-start | bytes 6291460
  320.9 4.2 %copy-start.6 = (f32[512,4,2,128]{3,0,2,1:T(8,128)S(1)}, f32[512,4,2,128]{3,0,2,1:T(8,128)}, u32[]{:S(2)}) copy-start(f32[512,4,2,128]{3,0,2,1:T(8,128)} %copy-done.5) | copy-start | bytes 6291460
  320.9 4.2 %copy-start.11 = (f32[4,8,128,128]{3,2,1,0:T(8,128)S(1)}, f32[4,8,128,128]{3,2,1,0:T(8,128)}, u32[]{:S(2)}) copy-start(f32[4,8,128,128]{3,2,1,0:T(8,128)} %get-tuple-element.120) | copy-start | bytes 6291460
  325.1 4.2 %copy-start.14 = (f32[128]{0:T(128)S(1)}, f32[128]{0:T(128)}, u32[]{:S(2)}) copy-start(f32[128]{0:T(128)} %param.19) | copy-start | bytes 1540
Sparse Core Ops, SparseCore 0:
  140.2 70.7 all-gather.4
  213.1 71.6 all-gather.6
